TPU v7x, 512 devices: a whole 4x8x8 slice. The times are simulated.
512 devices in a mesh: kv: 16 (over z, core), ep: 32 (over x, y).
Axes of the slice: x: 4, y: 8, z: 8, core: 2. Of those that a mesh axis runs over, the one named last changes fastest.
Arguments:
- queries: bfloat16 [32, 64, 2048], P('ep'), may hold values from -12 to 12
- new_keys: bfloat16 [32, 64, 512], P('ep'), may hold values from -12 to 12
- new_values: bfloat16 [32, 64, 512], P('ep'), may hold values from -6 to 6
- cache_keys: bfloat16 [32, 64, 128, 512], P('ep', 'kv'), may hold values from -12 to 12
- cache_values: bfloat16 [32, 64, 128, 512], P('ep', 'kv'), may hold values from -10 to 10
- page_table: int32 [32, 64], P('ep'), may hold values from 0 to 63, each once within a row
- cached_len: int32 [32], P('ep'), may hold values from 1 to 8192, 65536 in all
- moe_rows: bfloat16 [1024, 4096], P('ep'), may hold values from -6 to 6
- expert_ids: int32 [1024, 2], P('ep'), may hold values from 0 to 7, all different within a row; in each aligned block of 32 rows (0 to 31, 32 to 63, ...) at most 16 rows name the same one
- gate_probs: float32 [1024, 2], P('ep'), may hold values from 0.1 to 0.9
- w_gate: bfloat16 [32, 4096, 2048], P('ep', None, 'kv'), may hold values from -0.09375 to 0.09375
- w_up: bfloat16 [32, 4096, 2048], P('ep', None, 'kv'), may hold values from -0.09375 to 0.09375
- w_down: bfloat16 [32, 2048, 4096], P('ep', 'kv'), may hold values from -0.09375 to 0.09375
Outputs:
- attn_out: bfloat16 [32, 64, 2048], P('ep')
- moe_out: bfloat16 [1024, 4096], P('ep', 'kv')
Inputs may be any that keep to these rules, and one draw needn't show every extreme that they name: `page_table`: each row is a permutation of the 64 slots of its request. `cached_len`: cached positions at or past a request's length hold no data. `expert_ids`: each row names 2 different experts; among the 32 rows of one ep index no expert is named more than 16 times, and this bound is reached.
All inputs are finite; a program needn't handle non-finite values. No bound on the sum of `cached_len` on one device may be relied on, other than what follows from the above.
Results may differ from a plain program's by a relative error of at most 0.0085.
Values may be sent and summed in bfloat16 or wider, within the bound.
No kernel may reach another device: no remote copies, remote signals or barrier semaphores. Data moves between devices by JAX's collectives and lax.ppermute only.
A program may use at most 128 MiB of HBM per device.

v0:
```python
import math
import jax
import jax.numpy as jnp
from jax import lax
from jax.sharding import PartitionSpec as P

HD = 128
EXPERTS = 8
TOP = 2
HQ = 16
KVH = 4
PAGE = 128
POOL_DEV = 4
CAP = 16
ROPE_BASE = 10000.0
MASKED = -1e30


def rotary(values, positions):
    half_width = values.shape[-1] // 2
    indices = jnp.arange(half_width, dtype=jnp.float32)
    frequency = jnp.power(ROPE_BASE, -2.0 * indices / values.shape[-1])
    angles = positions.astype(jnp.float32)[:, None] * frequency[None, :]
    cosine = jnp.cos(angles)[:, None, :]
    sine_part = jnp.sin(angles)[:, None, :]
    lower_half = values[..., :half_width]
    upper_half = values[..., half_width:]
    return jnp.concatenate(
        [
            lower_half * cosine - upper_half * sine_part,
            upper_half * cosine + lower_half * sine_part,
        ],
        axis=-1,
    )


def on_device(
    queries,
    new_keys,
    new_values,
    cache_keys,
    cache_values,
    page_table,
    cached_len,
    moe_rows,
    expert_ids,
    gate_probs,
    w_gate,
    w_up,
    w_down,
):
    kv_index = lax.axis_index("kv")
    kv_count = lax.axis_size("kv")
    all_rows = queries.shape[1]
    block_rows = all_rows // kv_count
    length = cached_len[0]
    group_size = HQ // KVH
    score_scale = 1.0 / math.sqrt(HD)
    slot_ids = kv_index * POOL_DEV + jnp.arange(POOL_DEV, dtype=jnp.int32)
    matches = (page_table[0][:, None] == slot_ids[None, :]).astype(jnp.int32)
    page_index = jnp.sum(
        matches * jnp.arange(page_table.shape[1], dtype=jnp.int32)[:, None], axis=0
    )
    cached_pos = (page_index[:, None] * PAGE + jnp.arange(PAGE, dtype=jnp.int32)[None, :]).reshape(
        -1
    )
    block_start = kv_index * block_rows
    own_pos = length + block_start + jnp.arange(block_rows, dtype=jnp.int32)
    key_block = lax.dynamic_slice_in_dim(new_keys[0], block_start, block_rows, 0)
    value_block = lax.dynamic_slice_in_dim(new_values[0], block_start, block_rows, 0)
    own_keys = rotary(key_block.astype(jnp.float32).reshape(block_rows, KVH, HD), own_pos).astype(
        jnp.bfloat16
    )
    local_keys = jnp.concatenate([cache_keys[0].reshape(-1, KVH, HD), own_keys], axis=0)
    local_values = jnp.concatenate(
        [cache_values[0].reshape(-1, KVH, HD), value_block.reshape(block_rows, KVH, HD)], axis=0
    )
    key_pos = jnp.concatenate([cached_pos, own_pos])
    live_keys = jnp.concatenate([cached_pos < length, jnp.ones((block_rows,), jnp.bool_)])
    positions = length + jnp.arange(all_rows, dtype=jnp.int32)
    rotated = rotary(queries[0].astype(jnp.float32).reshape(all_rows, HQ, HD), positions).astype(
        jnp.bfloat16
    )
    grouped = rotated.reshape(all_rows, KVH, group_size, HD)
    scores = (
        jnp.einsum("nkgd,mkd->nkgm", grouped, local_keys, preferred_element_type=jnp.float32)
        * score_scale
    )
    usable = (live_keys[None, :] & (key_pos[None, :] <= positions[:, None]))[:, None, None, :]
    scores = jnp.where(usable, scores, MASKED)
    part_high = jnp.max(scores, axis=-1)
    highest = lax.pmax(part_high, "kv")
    weights = jnp.where(usable, jnp.exp(scores - highest[..., None]), 0.0)
    part_total = jnp.sum(weights, axis=-1)
    part_blend = jnp.einsum(
        "nkgm,mkd->nkgd",
        weights.astype(jnp.bfloat16),
        local_values,
        preferred_element_type=jnp.float32,
    )
    total_row = jnp.pad(part_total.reshape(1, -1), ((0, 0), (0, HQ * HD - all_rows * HQ)))
    packed = lax.psum(
        jnp.concatenate([part_blend.reshape(all_rows, HQ * HD), total_row], axis=0), "kv"
    )
    row_total = packed[all_rows, : all_rows * HQ].reshape(all_rows, HQ)
    blended = packed[:all_rows].reshape(all_rows, HQ, HD)
    attn_out = (blended / row_total[..., None]).reshape(1, all_rows, HQ * HD).astype(jnp.bfloat16)
    ep_count = lax.axis_size("ep")
    share_count = ep_count // EXPERTS
    tok_rows = moe_rows.shape[0]
    slot_total = ep_count * CAP
    flat_ids = expert_ids.reshape(-1)
    one_hot = (flat_ids[:, None] == jnp.arange(EXPERTS, dtype=jnp.int32)[None, :]).astype(jnp.int32)
    earlier = jnp.cumsum(one_hot, axis=0) - one_hot
    slot_rank = jnp.sum(earlier * one_hot, axis=1)
    slot_index = jnp.arange(slot_total, dtype=jnp.int32)
    dest_expert = slot_index // CAP // share_count
    dest_slot = slot_index % CAP
    matched = (flat_ids[None, :] == dest_expert[:, None]) & (
        slot_rank[None, :] == dest_slot[:, None]
    )
    select = jnp.sum(matched.astype(jnp.float32).reshape(slot_total, tok_rows, TOP), axis=2).astype(
        jnp.bfloat16
    )
    weight_map = jnp.sum(
        jnp.where(matched, gate_probs.reshape(-1)[None, :], 0.0).reshape(slot_total, tok_rows, TOP),
        axis=2,
    )
    col_width = moe_rows.shape[1] // kv_count
    rows_cols = lax.dynamic_slice_in_dim(moe_rows, kv_index * col_width, col_width, 1)
    outgoing = (
        jnp.dot(select, rows_cols, preferred_element_type=jnp.float32)
        .astype(jnp.bfloat16)
        .reshape(ep_count, CAP, -1)
    )
    arrived_cols = lax.all_to_all(outgoing, "ep", split_axis=0, concat_axis=0, tiled=True).reshape(
        slot_total, -1
    )
    arrived = lax.all_gather(arrived_cols, "kv", axis=1, tiled=True)
    gate_proj = jnp.dot(arrived, w_gate[0], preferred_element_type=jnp.float32)
    up_proj = jnp.dot(arrived, w_up[0], preferred_element_type=jnp.float32)
    hidden = (jax.nn.silu(gate_proj) * up_proj).astype(jnp.bfloat16)
    out_width = w_down.shape[2] // kv_count
    down_split = w_down[0].reshape(w_down.shape[1], kv_count, out_width)
    down_cols = lax.all_to_all(down_split, "kv", split_axis=1, concat_axis=0, tiled=True).reshape(
        -1, out_width
    )
    summed = jnp.dot(
        lax.all_gather(hidden, "kv", axis=1, tiled=True),
        down_cols,
        preferred_element_type=jnp.float32,
    )
    returned = (
        lax.all_to_all(
            summed.reshape(ep_count, CAP, -1).astype(jnp.bfloat16),
            "ep",
            split_axis=0,
            concat_axis=0,
            tiled=True,
        )
        .astype(jnp.float32)
        .reshape(slot_total, -1)
    )
    moe_out = jnp.dot(
        weight_map.T, returned, precision=lax.Precision.HIGHEST, preferred_element_type=jnp.float32
    ).astype(jnp.bfloat16)
    return (attn_out, moe_out)


def solution(mesh):
    return jax.shard_map(
        on_device,
        mesh=mesh,
        in_specs=(
            P("ep", None, None),
            P("ep", None, None),
            P("ep", None, None),
            P("ep", "kv", None, None),
            P("ep", "kv", None, None),
            P("ep", None),
            P("ep"),
            P("ep", None),
            P("ep", None),
            P("ep", None),
            P("ep", None, "kv"),
            P("ep", None, "kv"),
            P("ep", "kv", None),
        ),
        out_specs=(P("ep", None, None), P("ep", "kv")),
        check_vma=False,
    )
```

profile of v0, /device:TPU:2, one launch (start us, length us, event | category | flops | bytes accessed | tf_op | source)
XLA Modules:
  0.0 277.6 jit_solution(767339811898479776)
XLA Ops:
  7.2 0.0 copy-start
  7.2 0.0 all-gather.3.cloned.1.call-start
  7.2 0.8 copy.46
  8.1 0.1 eq.71
  8.2 0.1 fusion.26
  8.3 0.1 reduce_window_sum.11
  8.4 0.2 select_reduce_fusion.1
  8.5 0.1 eq.75
  8.7 0.1 copy.47
  8.7 0.8 convert_reduce_fusion
  9.6 1.0 convolution_convert_fusion
  10.5 21.4 %all_to_all.25 = bf16[32,16,256]{2,1,0:T(8,128)(2,1)} all-to-all(bf16[32,16,256]{2,1,0:T(8,128)(2,1)S(1)} %bitcast.94), channel_id=1, replica_groups=mesh['kv'=16,'ep'=32] {'ep'}, dimensions={0} | all-to-all | bytes 524288 | tf_op jit(solution)/shard_map/all_to_all | solution.py:136
  32.0 0.0 all-gather.3.cloned.1.call-update
  32.0 1.5 copy.55
  33.5 0.0 copy-start.4
  33.5 1.3 copy.48
  34.8 10.5 %all-to-all-start.1 = ((bf16[128,16,256]{2,0,1:T(8,128)(2,1)}), bf16[128,16,256]{2,0,1:T(8,128)(2,1)S(1)}, u32[]{:S(2)}, u32[]{:S(2)}) async-start(bf16[128,16,256]{2,0,1:T(8,128)(2,1)} %copy.48), calls=%async_computation.1 | async-start | bytes 2097152 | tf_op jit(solution)/shard_map/all_to_all | solution.py:145
  45.4 0.0 all-gather.5.cloned.1.call-start
  46.1 0.0 copy-done.4
  46.1 0.1 copy.53
  46.2 1.2 reshape_squeeze.10
  47.4 0.9 copy.41
  48.3 0.0 copy-done.6
  48.3 0.2 select_reduce_fusion.2
  48.5 55.1 %all-gather.3.cloned.1.call-done = bf16[512,4096]{1,0:T(8,128)(2,1)} async-done(((bf16[512,256]{1,0:T(8,128)(2,1)}), bf16[512,4096]{1,0:T(8,128)(2,1)}) %all-gather.3.cloned.1.call-update) | async-done | bytes 4194320 | tf_op jit(solution)/shard_map/all_gather | solution.py:139
  103.5 3.6 %fusion.11 = f32[512,128]{1,0:T(8,128)S(1)} fusion(bf16[512,4096]{1,0:T(8,128)(2,1)} %all-gather.3.cloned.1.call-done, bf16[1,4096,128]{2,1,0:T(8,128)(2,1)S(1)} %copy-done), kind=kOutput, calls=%fused_computation.14 | convolution fusion | flops 536870912 | bytes 5505024 | tf_op jit(solution)/shard_map/dot_general | solution.py:140
  107.1 0.1 copy-done.5
  107.3 1.9 fusion.9
  109.2 0.0 all-gather.5.cloned.1.call-update
  109.2 0.0 all-reduce.4.cloned.1.call-start
  109.3 0.1 broadcast_compare_fusion
  109.4 0.1 add_bitcast_fusion
  109.5 0.7 bitcast_convert_fusion
  110.2 0.1 multiply_cosine_fusion.1
  110.3 0.1 compare_and_fusion
  110.4 0.2 multiply_cosine_fusion
  110.6 0.1 subtract_convert_fusion.1
  110.7 0.2 fusion.48
  110.9 0.3 subtract_convert_fusion
  111.2 0.0 copy-start.2
  111.2 2.2 fusion
  113.5 24.3 %pmax.7 = f32[64,4,4]{0,2,1:T(4,128)S(1)} all-reduce(f32[64,4,4]{0,2,1:T(4,128)S(1)} %get-tuple-element.14), channel_id=1, replica_groups=mesh['kv'=16,'ep'=32] {'kv'}, use_global_device_ids=true, to_apply=%region_2.3 | all-reduce | flops 1024 | bytes 8192 | tf_op jit(solution)/shard_map/pmax | solution.py:92
  137.8 2.6 fusion.1
  140.4 0.1 copy.45
  140.5 0.2 reshape.299
  140.7 0.1 reshape_squeeze.9
  140.8 0.1 copy.40
  140.9 0.7 dynamic-slice_bitcast_fusion
  141.6 2.5 fusion.6
  144.1 0.3 copy.44
  144.5 0.2 reshape.298
  144.7 0.9 select_maximum_fusion
  145.6 0.0 all-reduce.4.cloned.1.call-update
  145.6 0.0 all-to-all-done.1
  145.6 3.0 %all-gather.5.cloned.1.call-done = bf16[512,2048]{1,0:T(8,128)(2,1)} async-done(((bf16[512,128]{1,0:T(8,128)(2,1)}), bf16[512,2048]{1,0:T(8,128)(2,1)}) %all-gather.5.cloned.1.call-update) | async-done | bytes 2097168 | tf_op jit(solution)/shard_map/all_gather | solution.py:149
  148.6 3.0 %convolution_convert_fusion.1 = bf16[32,16,256]{2,1,0:T(8,128)(2,1)} fusion(bf16[32,16,2048]{2,1,0:T(8,128)(2,1)} %bitcast.97, bf16[2048,256,1]{1,0,2:T(8,128)(2,1)S(1)} %bitcast.91), kind=kOutput, calls=%fused_computation.9 | convolution fusion | flops 537001984 | bytes 3407872 | tf_op jit(solution)/shard_map/dot_general | solution.py:148
  151.6 9.9 %all-to-all-start.2 = ((bf16[32,16,256]{2,1,0:T(8,128)(2,1)}), bf16[32,16,256]{2,1,0:T(8,128)(2,1)S(1)}, u32[]{:S(2)}, u32[]{:S(2)}) async-start(bf16[32,16,256]{2,1,0:T(8,128)(2,1)} %convolution_convert_fusion.1), calls=%async_computation.2 | async-start | bytes 524288 | tf_op jit(solution)/shard_map/all_to_all | solution.py:154
  161.5 105.7 %all-reduce.4.cloned.1.call-done = f32[65,2048]{1,0:T(8,128)} async-done(((f32[65,2048]{1,0:T(8,128)}), f32[65,2048]{1,0:T(8,128)}) %all-reduce.4.cloned.1.call-update) | async-done | bytes 532496 | tf_op jit(solution)/shard_map/psum | solution.py:102
  267.2 0.8 slice_reduce_fusion
  268.0 0.1 div.45
  268.0 0.2 div.46
  268.2 1.9 fusion.24
  270.2 0.0 all-to-all-done.2
  270.2 0.9 convolution_convert_fusion.2
  (17 shorter events, 0.1 us)
Async XLA Ops:
  7.2 96.4 %copy-start = (bf16[1,4096,128]{2,1,0:T(8,128)(2,1)S(1)}, bf16[1,4096,128]{2,1,0:T(8,128)(2,1)}, u32[]{:S(2)}) copy-start(bf16[1,4096,128]{2,1,0:T(8,128)(2,1)} %param.23) | copy-start | bytes 3145732
  7.2 96.3 %all-gather.3.cloned.1.call-start = ((), (), s32[]{:S(2)}) async-start(), calls=%async_computation.4 | async-start | bytes 4456448 | tf_op jit(solution)/shard_map/all_gather | solution.py:139
  33.5 12.6 %copy-start.4 = (bf16[1,64,2048]{2,1,0:T(8,128)(2,1)S(1)}, bf16[1,64,2048]{2,1,0:T(8,128)(2,1)}, u32[]{:S(2)}) copy-start(bf16[1,64,2048]{2,1,0:T(8,128)(2,1)} %param.13) | copy-start | bytes 786436
  34.8 13.5 %copy-start.6 = (s32[1,64]{1,0:T(1,128)S(1)}, s32[1,64]{1,0:T(1,128)}, u32[]{:S(2)}) copy-start(s32[1,64]{1,0:T(1,128)} %param.18) | copy-start | bytes 772
  34.8 110.8 %all-to-all-start.1 = ((bf16[128,16,256]{2,0,1:T(8,128)(2,1)}), bf16[128,16,256]{2,0,1:T(8,128)(2,1)S(1)}, u32[]{:S(2)}, u32[]{:S(2)}) async-start(bf16[128,16,256]{2,0,1:T(8,128)(2,1)} %copy.48), calls=%async_computation.1 | async-start | bytes 2097152 | tf_op jit(solution)/shard_map/all_to_all | solution.py:145
  45.4 103.2 %all-gather.5.cloned.1.call-start = ((), (), s32[]{:S(2)}) async-start(), calls=%async_computation.5 | async-start | bytes 2228224 | tf_op jit(solution)/shard_map/all_gather | solution.py:149
  103.5 3.6 %copy-start.1 = (bf16[512,4096]{1,0:T(8,128)(2,1)S(1)}, bf16[512,4096]{1,0:T(8,128)(2,1)}, u32[]{:S(2)}) copy-start(bf16[512,4096]{1,0:T(8,128)(2,1)} %all-gather.3.cloned.1.call-done) | copy-start | bytes 12582916
  103.5 3.7 %copy-start.5 = (bf16[1,4096,128]{2,1,0:T(8,128)(2,1)S(1)}, bf16[1,4096,128]{2,1,0:T(8,128)(2,1)}, u32[]{:S(2)}) copy-start(bf16[1,4096,128]{2,1,0:T(8,128)(2,1)} %param.24) | copy-start | bytes 3145732
  109.2 2.0 copy-start.3
  109.2 158.0 %all-reduce.4.cloned.1.call-start = ((), (), s32[]{:S(2)}) async-start(), calls=%async_computation.3 | async-start | bytes 1179648 | tf_op jit(solution)/shard_map/psum | solution.py:102
  111.2 29.5 %copy-start.2 = (bf16[1,4,128,512]{3,2,1,0:T(8,128)(2,1)S(1)}, bf16[1,4,128,512]{3,2,1,0:T(8,128)(2,1)}, u32[]{:S(2)}) copy-start(bf16[1,4,128,512]{3,2,1,0:T(8,128)(2,1)} %param.17) | copy-start | bytes 1572868
  151.6 118.6 %all-to-all-start.2 = ((bf16[32,16,256]{2,1,0:T(8,128)(2,1)}), bf16[32,16,256]{2,1,0:T(8,128)(2,1)S(1)}, u32[]{:S(2)}, u32[]{:S(2)}) async-start(bf16[32,16,256]{2,1,0:T(8,128)(2,1)} %convolution_convert_fusion.1), calls=%async_computation.2 | async-start | bytes 524288 | tf_op jit(solution)/shard_map/all_to_all | solution.py:154
Sparse Core Ops, SparseCore 0:
  32.1 71.3 all-gather.2
  109.3 39.2 all-gather.4
  150.9 116.2 all-reduce.3
where the time goes:
time: 278 us
  waiting for transfers between devices  164 us (59%)
  blocking collectives  45.7 us (16%)
  starting transfers between devices  20.6 us (7%)
  matrix products  15 us (5%)
  between operations  14.7 us (5%)
  local copies, waits for them, and re-layouts  9.25 us (3%)
  other arithmetic  8.53 us (3%)
    psum x1, waiting for transfers between devices, on_device(): lax.psum(jnp.concatenate([part_blend.reshape(all_rows, HQ * HD), total_ro...  106 us
    all_gather x1, waiting for transfers between devices, on_device(): arrived = lax.all_gather(arrived_cols, 'kv', axis=1, tiled=True)  55.1 us
    pmax x1, blocking collectives, on_device(): highest = lax.pmax(part_high, 'kv')  24.3 us
    all_to_all x1, blocking collectives, on_device(): lax.all_to_all(outgoing, 'ep', split_axis=0, concat_axis=0, tiled=True)  21.4 us
    all_to_all x1, starting transfers between devices, on_device(): lax.all_to_all(down_split, 'kv', split_axis=1, concat_axis=0, tiled=True)  10.5 us
    all_to_all x1, starting transfers between devices, on_device(): lax.all_to_all(summed.reshape(ep_count, CAP, -1).astype(jnp.bfloat16), 'e...  9.89 us
  transfers between devices with their start and end apart: 5, of which 3 were waited for; matrix products, arithmetic and copies ran while one was open for 10% of the time, Pallas kernels for 0%

commit v1 on v0

--- a/solution.py
+++ b/solution.py
@@ -142,9 +142,10 @@
     hidden = (jax.nn.silu(gate_proj) * up_proj).astype(jnp.bfloat16)
     out_width = w_down.shape[2] // kv_count
     down_split = w_down[0].reshape(w_down.shape[1], kv_count, out_width)
-    down_cols = lax.all_to_all(down_split, "kv", split_axis=1, concat_axis=0, tiled=True).reshape(
-        -1, out_width
-    )
+    down_cols = jnp.concatenate(
+        lax.all_to_all(jnp.stack(jnp.split(down_split, lax.axis_size("kv"), axis=1)), "kv", 0, 0),
+        axis=0,
+    ).reshape(-1, out_width)
     summed = jnp.dot(
         lax.all_gather(hidden, "kv", axis=1, tiled=True),
         down_cols,

time: 278 us -> 277 us (level)
  no operation moved by 1% of the time
where the time goes in v1:
time: 277 us; the launch traced here: 276 us
  waiting for transfers between devices  162 us (58%)
  blocking collectives  46.5 us (17%)
  starting transfers between devices  20.5 us (7%)
  matrix products  15 us (5%)
  between operations  14.8 us (5%)
  local copies, waits for them, and re-layouts  9.62 us (3%)
  other arithmetic  8.52 us (3%)
    psum x1, waiting for transfers between devices, on_device(): lax.psum(jnp.concatenate([part_blend.reshape(all_rows, HQ * HD), total_ro...  105 us
    all_gather x1, waiting for transfers between devices, on_device(): arrived = lax.all_gather(arrived_cols, 'kv', axis=1, tiled=True)  54.8 us
    pmax x1, blocking collectives, on_device(): highest = lax.pmax(part_high, 'kv')  25.1 us
    all_to_all x1, blocking collectives, on_device(): lax.all_to_all(outgoing, 'ep', split_axis=0, concat_axis=0, tiled=True)  21.4 us
    all_to_all x1, starting transfers between devices, on_device(): lax.all_to_all(jnp.stack(jnp.split(down_split, lax.axis_size('kv'), axis=...  10.5 us
    all_to_all x1, starting transfers between devices, on_device(): lax.all_to_all(summed.reshape(ep_count, CAP, -1).astype(jnp.bfloat16), 'e...  9.8 us
  transfers between devices with their start and end apart: 5, of which 3 were waited for; matrix products, arithmetic and copies ran while one was open for 10% of the time, Pallas kernels for 0%

profile of v1, /device:TPU:2, one launch (start us, length us, event | category | flops | bytes accessed | tf_op | source)
XLA Modules:
  0.0 276.5 jit_solution(16565439048841786690)
XLA Ops:
  7.2 0.0 copy-start
  7.2 0.0 all-gather.3.cloned.1.call-start
  7.2 0.8 copy.86
  8.1 0.1 eq.71
  8.2 0.1 fusion.42
  8.3 0.1 reduce_window_sum.11
  8.4 0.2 select_reduce_fusion.1
  8.5 0.1 eq.75
  8.7 0.1 copy.87
  8.7 0.8 convert_reduce_fusion
  9.6 1.0 convolution_convert_fusion
  10.5 21.4 %all_to_all.15 = bf16[32,16,256]{2,1,0:T(8,128)(2,1)} all-to-all(bf16[32,16,256]{2,1,0:T(8,128)(2,1)S(1)} %bitcast.166), channel_id=1, replica_groups=mesh['kv'=16,'ep'=32] {'ep'}, dimensions={0} | all-to-all | bytes 524288 | tf_op jit(solution)/shard_map/all_to_all | solution.py:136
  32.0 0.0 all-gather.3.cloned.1.call-update
  32.0 1.6 copy.88
  33.8 0.0 copy-start.4
  33.9 1.3 copy.89
  35.2 10.5 %all-to-all-start.1 = ((bf16[16,128,1,256]{3,1,2,0:T(8,128)(2,1)}), bf16[16,128,1,256]{3,1,2,0:T(8,128)(2,1)S(1)}, u32[]{:S(2)}, u32[]{:S(2)}) async-start(bf16[16,128,1,256]{3,1,2,0:T(8,128)(2,1)} %copy.89), calls=%async_computation.1 | async-start | bytes 2097152 | tf_op jit(solution)/shard_map/all_to_all | solution.py:146
  45.8 0.0 all-gather.5.cloned.1.call-start
  46.5 0.0 copy-done.4
  46.6 0.1 copy.94
  46.7 1.2 reshape_squeeze.10
  47.8 0.9 copy.81
  48.7 0.2 select_reduce_fusion.2
  48.9 54.8 %all-gather.3.cloned.1.call-done = bf16[512,4096]{1,0:T(8,128)(2,1)} async-done(((bf16[512,256]{1,0:T(8,128)(2,1)}), bf16[512,4096]{1,0:T(8,128)(2,1)}) %all-gather.3.cloned.1.call-update) | async-done | bytes 4194320 | tf_op jit(solution)/shard_map/all_gather | solution.py:139
  103.7 0.0 copy-done
  103.7 3.6 %fusion.11 = f32[512,128]{1,0:T(8,128)S(1)} fusion(bf16[512,4096]{1,0:T(8,128)(2,1)} %all-gather.3.cloned.1.call-done, bf16[1,4096,128]{2,1,0:T(8,128)(2,1)S(1)} %copy-done), kind=kOutput, calls=%fused_computation.14 | convolution fusion | flops 536870912 | bytes 5505024 | tf_op jit(solution)/shard_map/dot_general | solution.py:140
  107.3 0.1 copy-done.5
  107.5 1.9 fusion.9
  109.4 0.0 all-gather.5.cloned.1.call-update
  109.4 0.0 all-reduce.4.cloned.1.call-start
  109.4 0.1 broadcast_compare_fusion
  109.6 0.1 add_bitcast_fusion
  109.6 0.7 bitcast_convert_fusion
  110.3 0.1 multiply_cosine_fusion.1
  110.5 0.1 compare_and_fusion
  110.6 0.2 multiply_cosine_fusion
  110.8 0.1 subtract_convert_fusion.1
  110.8 0.2 fusion.64
  111.0 0.3 subtract_convert_fusion
  111.4 0.0 copy-start.2
  111.4 2.2 fusion
  113.6 25.1 %pmax.7 = f32[64,4,4]{0,2,1:T(4,128)S(1)} all-reduce(f32[64,4,4]{0,2,1:T(4,128)S(1)} %get-tuple-element.14), channel_id=1, replica_groups=mesh['kv'=16,'ep'=32] {'kv'}, use_global_device_ids=true, to_apply=%region_2.3 | all-reduce | flops 1024 | bytes 8192 | tf_op jit(solution)/shard_map/pmax | solution.py:92
  138.7 2.6 fusion.1
  141.3 0.1 copy.85
  141.5 0.2 reshape.295
  141.6 0.1 reshape_squeeze.9
  141.8 0.1 copy.80
  141.9 0.7 dynamic-slice_bitcast_fusion
  142.6 2.5 fusion.6
  145.1 0.3 copy.84
  145.4 0.2 reshape.294
  145.7 0.9 select_maximum_fusion
  146.5 0.0 all-reduce.4.cloned.1.call-update
  146.5 0.0 all-to-all-done.1
  146.5 1.4 all-gather.5.cloned.1.call-done
  147.9 3.0 %convolution_convert_fusion.1 = bf16[32,16,256]{2,1,0:T(8,128)(2,1)} fusion(bf16[32,16,2048]{2,1,0:T(8,128)(2,1)} %bitcast.169, bf16[2048,256,1]{1,0,2:T(8,128)(2,1)S(1)} %bitcast.163), kind=kOutput, calls=%fused_computation.9 | convolution fusion | flops 537001984 | bytes 3407872 | tf_op jit(solution)/shard_map/dot_general | solution.py:149
  150.9 9.8 %all-to-all-start.2 = ((bf16[32,16,256]{2,1,0:T(8,128)(2,1)}), bf16[32,16,256]{2,1,0:T(8,128)(2,1)S(1)}, u32[]{:S(2)}, u32[]{:S(2)}) async-start(bf16[32,16,256]{2,1,0:T(8,128)(2,1)} %convolution_convert_fusion.1), calls=%async_computation.2 | async-start | bytes 524288 | tf_op jit(solution)/shard_map/all_to_all | solution.py:155
  160.7 105.4 %all-reduce.4.cloned.1.call-done = f32[65,2048]{1,0:T(8,128)} async-done(((f32[65,2048]{1,0:T(8,128)}), f32[65,2048]{1,0:T(8,128)}) %all-reduce.4.cloned.1.call-update) | async-done | bytes 532496 | tf_op jit(solution)/shard_map/psum | solution.py:102
  266.1 0.8 slice_reduce_fusion
  266.9 0.1 div.45
  267.0 0.2 div.46
  267.2 1.9 fusion.24
  269.1 0.0 all-to-all-done.2
  269.1 0.9 convolution_convert_fusion.2
  (33 shorter events, 0.3 us)
Async XLA Ops:
  7.2 96.5 %copy-start = (bf16[1,4096,128]{2,1,0:T(8,128)(2,1)S(1)}, bf16[1,4096,128]{2,1,0:T(8,128)(2,1)}, u32[]{:S(2)}) copy-start(bf16[1,4096,128]{2,1,0:T(8,128)(2,1)} %param.23) | copy-start | bytes 3145732
  7.2 96.5 %all-gather.3.cloned.1.call-start = ((), (), s32[]{:S(2)}) async-start(), calls=%async_computation.4 | async-start | bytes 4456448 | tf_op jit(solution)/shard_map/all_gather | solution.py:139
  33.8 12.8 %copy-start.4 = (bf16[1,64,2048]{2,1,0:T(8,128)(2,1)S(1)}, bf16[1,64,2048]{2,1,0:T(8,128)(2,1)}, u32[]{:S(2)}) copy-start(bf16[1,64,2048]{2,1,0:T(8,128)(2,1)} %param.13) | copy-start | bytes 786436
  35.2 13.5 %copy-start.6 = (s32[1,64]{1,0:T(1,128)S(1)}, s32[1,64]{1,0:T(1,128)}, u32[]{:S(2)}) copy-start(s32[1,64]{1,0:T(1,128)} %param.18) | copy-start | bytes 772
  35.2 111.3 %all-to-all-start.1 = ((bf16[16,128,1,256]{3,1,2,0:T(8,128)(2,1)}), bf16[16,128,1,256]{3,1,2,0:T(8,128)(2,1)S(1)}, u32[]{:S(2)}, u32[]{:S(2)}) async-start(bf16[16,128,1,256]{3,1,2,0:T(8,128)(2,1)} %copy.89), calls=%async_computation.1 | async-start | bytes 2097152 | tf_op jit(solution)/shard_map/all_to_all | solution.py:146
  45.8 102.1 %all-gather.5.cloned.1.call-start = ((), (), s32[]{:S(2)}) async-start(), calls=%async_computation.5 | async-start | bytes 2228224 | tf_op jit(solution)/shard_map/all_gather | solution.py:150
  103.7 3.6 %copy-start.1 = (bf16[512,4096]{1,0:T(8,128)(2,1)S(1)}, bf16[512,4096]{1,0:T(8,128)(2,1)}, u32[]{:S(2)}) copy-start(bf16[512,4096]{1,0:T(8,128)(2,1)} %all-gather.3.cloned.1.call-done) | copy-start | bytes 12582916
  103.7 3.7 %copy-start.5 = (bf16[1,4096,128]{2,1,0:T(8,128)(2,1)S(1)}, bf16[1,4096,128]{2,1,0:T(8,128)(2,1)}, u32[]{:S(2)}) copy-start(bf16[1,4096,128]{2,1,0:T(8,128)(2,1)} %param.24) | copy-start | bytes 3145732
  109.4 2.0 copy-start.3
  109.4 156.7 %all-reduce.4.cloned.1.call-start = ((), (), s32[]{:S(2)}) async-start(), calls=%async_computation.3 | async-start | bytes 1179648 | tf_op jit(solution)/shard_map/psum | solution.py:102
  111.4 30.2 %copy-start.2 = (bf16[1,4,128,512]{3,2,1,0:T(8,128)(2,1)S(1)}, bf16[1,4,128,512]{3,2,1,0:T(8,128)(2,1)}, u32[]{:S(2)}) copy-start(bf16[1,4,128,512]{3,2,1,0:T(8,128)(2,1)} %param.17) | copy-start | bytes 1572868
  150.9 118.2 %all-to-all-start.2 = ((bf16[32,16,256]{2,1,0:T(8,128)(2,1)}), bf16[32,16,256]{2,1,0:T(8,128)(2,1)S(1)}, u32[]{:S(2)}, u32[]{:S(2)}) async-start(bf16[32,16,256]{2,1,0:T(8,128)(2,1)} %convolution_convert_fusion.1), calls=%async_computation.2 | async-start | bytes 524288 | tf_op jit(solution)/shard_map/all_to_all | solution.py:155
Sparse Core Ops, SparseCore 0:
  32.1 71.5 all-gather.2
  109.5 38.3 all-gather.4
  150.3 115.7 all-reduce.3
